TPU v7x, 512 devices: a whole 4x8x8 slice. The times are simulated.
512 devices in a mesh: dp: 2 (over core), section: 4 (over x), expert: 64 (over y, z).
Axes of the slice: x: 4, y: 8, z: 8, core: 2. Of those that a mesh axis runs over, the one named last changes fastest.
Arguments:
- grad_out: bfloat16 [16384, 3584], P(('dp', 'expert'), 'section'), may hold values from -6 to 6
- expert_ids: int32 [16384, 8], P(('dp', 'expert')), may hold values from 0 to 63, all different within a row; in each aligned block of 128 rows (0 to 127, 128 to 255, ...) at most 24 rows name the same one
- gate_weights: float32 [16384, 8], P(('dp', 'expert')), may hold values from 0.1 to 1
- act: bfloat16 [16384, 8, 1024], P(('dp', 'expert'), None, 'section'), may hold values from -0.8984375 to 0.8984375
- w_down: bfloat16 [64, 1024, 3584], P('expert', 'section'), may hold values from -0.09375 to 0.09375
Outputs:
- grad_hidden: bfloat16 [16384, 8, 1024], P(('dp', 'expert'), None, 'section')
- grad_gates: float32 [16384, 8], P(('dp', 'expert'))
- grad_w: bfloat16 [64, 1024, 3584], P('expert', 'section', 'dp')
Inputs may be any that keep to these rules, and one draw needn't show every extreme that they name: `expert_ids`: each row names 8 different experts. In each aligned block of 128 rows (the tokens of one device) no expert is named by more than 24 rows, and in every draw some expert is named by exactly 24 rows of some block.
All inputs are finite; a program needn't handle non-finite values.
Results may differ from a plain program's by a relative error of at most 0.0058.
Values may be sent and summed in bfloat16 or wider, within the bound.
No kernel may reach another device: no remote copies, remote signals or barrier semaphores. Data moves between devices by JAX's collectives and lax.ppermute only.
A program may use at most 64 MiB of HBM per device.

v0:
```python
import jax
import jax.numpy as jnp
from jax import lax
from jax.sharding import PartitionSpec as P


def routing(expert_ids, experts, capacity):
    tok_count, top_count = expert_ids.shape
    onehot = expert_ids[:, :, None] == jnp.arange(experts, dtype=jnp.int32)[None, None, :]
    per_token = jnp.any(onehot, axis=1).astype(jnp.bfloat16)
    rows = jnp.arange(tok_count, dtype=jnp.int32)
    lower = (rows[:, None] > rows[None, :]).astype(jnp.bfloat16)
    before = jnp.dot(lower, per_token, preferred_element_type=jnp.float32)
    order_in = jnp.sum(jnp.where(onehot, before[:, None, :], 0.0), axis=2).astype(jnp.int32)
    position = expert_ids * capacity + order_in
    slots = jnp.arange(experts * capacity, dtype=jnp.int32)
    sel_pairs = position.reshape(tok_count * top_count)[None, :] == slots[:, None]
    sel_tok = jnp.any(position[None, :, :] == slots[:, None, None], axis=2)
    return (sel_pairs.astype(jnp.bfloat16), sel_tok.astype(jnp.bfloat16))


def local(grad_out, expert_ids, gate_weights, act, w_down):
    tok_count, top_count = expert_ids.shape
    hidden_slice = act.shape[2]
    d_slice = grad_out.shape[1]
    n_expert = lax.axis_size("expert")
    n_section = lax.axis_size("section")
    experts = w_down.shape[0] * n_expert
    capacity = 3 * tok_count * top_count // (2 * experts)
    pair_count = tok_count * top_count
    slot_count = experts * capacity
    sel_pairs, sel_tok = routing(expert_ids, experts, capacity)
    scaled = (
        (gate_weights[:, :, None] * act.astype(jnp.float32))
        .astype(jnp.bfloat16)
        .reshape(pair_count, hidden_slice)
    )
    send_scaled = jnp.dot(sel_pairs, scaled, preferred_element_type=jnp.float32).astype(
        jnp.bfloat16
    )
    send_grad = jnp.dot(sel_tok, grad_out, preferred_element_type=jnp.float32).astype(jnp.bfloat16)
    send = jnp.concatenate([send_grad, send_scaled], axis=1).reshape(
        experts, capacity, d_slice + hidden_slice
    )
    recv = lax.all_to_all(send, "expert", split_axis=0, concat_axis=0, tiled=True)
    recv = recv.reshape(slot_count, d_slice + hidden_slice)
    recv_grad = recv[:, :d_slice]
    recv_scaled = recv[:, d_slice:]
    spread = jnp.broadcast_to(recv_grad[None], (n_section, slot_count, d_slice))
    gathered = lax.all_to_all(spread, "section", split_axis=0, concat_axis=0, tiled=True)
    w_local = w_down[0].reshape(hidden_slice, n_section, d_slice)
    unscaled = jnp.einsum("srd,hsd->rh", gathered, w_local, preferred_element_type=jnp.float32)
    weight_part = (
        jnp.einsum("rh,srd->hsd", recv_scaled, gathered, preferred_element_type=jnp.float32)
        .astype(jnp.bfloat16)
        .reshape(1, hidden_slice, n_section * d_slice)
    )
    grad_w = lax.psum_scatter(weight_part, "dp", scatter_dimension=2, tiled=True)
    returning = unscaled.astype(jnp.bfloat16).reshape(experts, capacity, hidden_slice)
    returned = lax.all_to_all(returning, "expert", split_axis=0, concat_axis=0, tiled=True)
    unscaled_tok = lax.dot_general(
        sel_pairs,
        returned.reshape(slot_count, hidden_slice),
        (((0,), (0,)), ((), ())),
        preferred_element_type=jnp.float32,
    ).reshape(tok_count, top_count, hidden_slice)
    grad_hidden = (gate_weights[:, :, None] * unscaled_tok).astype(jnp.bfloat16)
    gate_share = jnp.sum(act.astype(jnp.float32) * unscaled_tok, axis=2)
    grad_gates = lax.psum(gate_share, "section")
    return (grad_hidden, grad_gates, grad_w)


def solution(mesh):
    placed = (
        P(("dp", "expert"), "section"),
        P(("dp", "expert"), None),
        P(("dp", "expert"), None),
        P(("dp", "expert"), None, "section"),
        P("expert", "section", None),
    )
    return jax.shard_map(
        local,
        mesh=mesh,
        in_specs=placed,
        out_specs=(
            P(("dp", "expert"), None, "section"),
            P(("dp", "expert"), None),
            P("expert", "section", "dp"),
        ),
        check_vma=False,
    )
```

profile of v0, /device:TPU:16, one launch (start us, length us, event | category | flops | bytes accessed | tf_op | source)
XLA Modules:
  0.0 339.1 jit_solution(5224360648791601588)
XLA Ops:
  7.2 0.0 copy-start
  7.2 0.0 copy-start.5
  7.2 0.0 copy-start.4
  7.2 0.0 reduce-scatter.2.cloned.1.call-start
  7.2 0.8 fusion.14
  8.1 0.1 fusion.15
  8.2 0.7 select_reduce_fusion
  9.0 0.7 convert_add_fusion
  9.6 5.6 %fusion.3 = pred[1536,128]{1,0:T(8,128)(4,1)S(1)} fusion(s32[128,8]{0,1:T(8,128)S(1)} %convert_add_fusion), kind=kLoop, calls=%fused_computation.5 | loop fusion | flops 2949120 | bytes 200704 | tf_op jit(solution)/shard_map/reduce_or | solution.py:18
  15.2 0.1 copy.27
  15.3 0.1 eq.70
  15.4 0.0 copy-done
  15.4 0.9 convolution_convert_fusion
  16.4 0.0 copy-done.5
  16.4 0.0 copy-done.4
  16.4 0.2 fusion.10
  16.6 1.6 fusion.8
  18.2 2.0 pad_maximum_fusion
  20.2 5.8 %copy.30 = bf16[1536,1152]{1,0:T(8,128)(2,1)} copy(bf16[1536,1152]{0,1:T(8,128)(2,1)} %pad_maximum_fusion) | data formatting | bytes 7077888 | tf_op jit(solution)/shard_map/concatenate | solution.py:42
  26.0 99.0 %all_to_all.15 = bf16[64,24,1152]{2,1,0:T(8,128)(2,1)S(1)} all-to-all(bf16[64,24,1152]{2,1,0:T(8,128)(2,1)} %bitcast.29), channel_id=1, replica_groups=mesh['dp'=2,'section'=4,'expert'=64] {'expert'}, dimensions={0} | all-to-all | bytes 7077888 | tf_op jit(solution)/shard_map/all_to_all | solution.py:45
  125.0 0.0 copy-start.1
  125.0 1.9 copy-done.1
  126.8 0.2 slice.8
  127.0 5.0 %broadcast_in_dim.16 = bf16[4,1536,896]{2,1,0:T(8,128)(2,1)} broadcast(bf16[1536,896]{1,0:T(8,128)(2,1)S(1)} %slice.8), dimensions={1,2} | broadcast | bytes 13762560 | tf_op jit(solution)/shard_map/broadcast_in_dim | solution.py:49
  132.0 125.3 %all_to_all.16 = bf16[4,1536,896]{2,1,0:T(8,128)(2,1)S(1)} all-to-all(bf16[4,1536,896]{2,1,0:T(8,128)(2,1)} %broadcast_in_dim.16), channel_id=1, replica_groups=mesh['dp'=2,'section'=4,'expert'=64] {'section'}, dimensions={0} | all-to-all | bytes 22020096 | tf_op jit(solution)/shard_map/all_to_all | solution.py:50
  257.4 0.0 copy-start.2
  257.4 4.2 %copy-done.2 = bf16[4,1536,896]{2,1,0:T(8,128)(2,1)} copy-done((bf16[4,1536,896]{2,1,0:T(8,128)(2,1)}, bf16[4,1536,896]{2,1,0:T(8,128)(2,1)S(1)}, u32[]{:S(2)}) %copy-start.2) | copy-done | bytes 11010072
  261.5 5.3 %convolution_convert_fusion.1 = bf16[256,4,896]{2,0,1:T(8,128)(2,1)} fusion(bf16[4,1536,896]{2,1,0:T(8,128)(2,1)S(1)} %all_to_all.16, bf16[1536,1152]{1,0:T(8,128)(2,1)} %bitcast.31), kind=kOutput, calls=%fused_computation.15 | convolution fusion | flops 2819489792 | bytes 13631488 | tf_op jit(solution)/shard_map/rh,srd->hsd/dot_general | solution.py:54
  266.8 0.0 copy-start.3
  266.8 3.7 %copy.33 = bf16[256,4,896]{0,2,1:T(8,128)(2,1)} copy(bf16[256,4,896]{2,0,1:T(8,128)(2,1)} %convolution_convert_fusion.1) | data formatting | bytes 3670016 | tf_op jit(solution)/shard_map/convert_element_type | solution.py:55
  270.5 0.0 reduce-scatter.2.cloned.1.call-update
  270.6 0.0 copy-done.3
  270.6 1.5 reshape_squeeze.3
  272.1 7.7 %fusion.7 = bf16[1536,256]{1,0:T(8,128)(2,1)S(1)} fusion(bf16[4,1536,896]{2,1,0:T(8,128)(2,1)} %copy-done.2, bf16[256,4,896]{2,1,0:T(4,128)(2,1)} %reshape_squeeze.3), kind=kOutput, calls=%fused_computation.12 | convolution fusion | flops 2818965504 | bytes 13631488 | tf_op jit(solution)/shard_map/srd,hsd->rh/dot_general | solution.py:52
  279.8 38.6 %all_to_all.17 = bf16[64,24,256]{2,1,0:T(8,128)(2,1)S(1)} all-to-all(bf16[64,24,256]{2,1,0:T(8,128)(2,1)S(1)} %bitcast.34), channel_id=1, replica_groups=mesh['dp'=2,'section'=4,'expert'=64] {'expert'}, dimensions={0} | all-to-all | bytes 1572864 | tf_op jit(solution)/shard_map/all_to_all | solution.py:60
  318.4 1.4 fusion.11
  319.8 1.1 copy.34
  320.9 9.2 %psum.7 = f32[128,8]{0,1:T(8,128)} all-reduce(f32[128,8]{0,1:T(8,128)S(1)} %get-tuple-element.12), channel_id=1, replica_groups=mesh['dp'=2,'section'=4,'expert'=64] {'section'}, use_global_device_ids=true, to_apply=%region_4.5 | all-reduce | flops 1024 | bytes 8192 | tf_op jit(solution)/shard_map/psum | solution.py:69
  330.1 0.0 reduce-scatter.2.cloned.1.call-done
  330.1 2.2 copy.35
Async XLA Ops:
  7.2 8.3 %copy-start = (bf16[128,896]{1,0:T(8,128)(2,1)S(1)}, bf16[128,896]{1,0:T(8,128)(2,1)}, u32[]{:S(2)}) copy-start(bf16[128,896]{1,0:T(8,128)(2,1)} %param.5) | copy-start | bytes 688132
  7.2 9.2 %copy-start.5 = (f32[128,8]{0,1:T(8,128)S(1)}, f32[128,8]{0,1:T(8,128)}, u32[]{:S(2)}) copy-start(f32[128,8]{0,1:T(8,128)} %param.7) | copy-start | bytes 12292
  7.2 9.2 %copy-start.4 = (bf16[128,8,256]{2,1,0:T(8,128)(2,1)S(1)}, bf16[128,8,256]{2,1,0:T(8,128)(2,1)}, u32[]{:S(2)}) copy-start(bf16[128,8,256]{2,1,0:T(8,128)(2,1)} %param.8) | copy-start | bytes 1572868
  7.2 322.9 %reduce-scatter.2.cloned.1.call-start = ((), (), s32[]{:S(2)}) async-start(), calls=%async_computation.4 | async-start | bytes 2752512 | tf_op jit(solution)/shard_map/reduce_scatter | solution.py:58
  125.0 1.9 copy-start.1
  257.4 4.2 %copy-start.2 = (bf16[4,1536,896]{2,1,0:T(8,128)(2,1)}, bf16[4,1536,896]{2,1,0:T(8,128)(2,1)S(1)}, u32[]{:S(2)}) copy-start(bf16[4,1536,896]{2,1,0:T(8,128)(2,1)S(1)} %all_to_all.16) | copy-start | bytes 33030148
  266.8 3.7 %copy-start.3 = (bf16[1,256,3584]{2,1,0:T(8,128)(2,1)S(1)}, bf16[1,256,3584]{2,1,0:T(8,128)(2,1)}, u32[]{:S(2)}) copy-start(bf16[1,256,3584]{2,1,0:T(8,128)(2,1)} %param.9) | copy-start | bytes 5505028
Sparse Core Ops, SparseCore 0:
  270.7 19.9 reduce-scatter.1
where the time goes:
time: 340 us; the launch traced here: 339 us
  blocking collectives  272 us (80%)
  local copies, waits for them, and re-layouts  25.7 us (8%)
  matrix products  17.1 us (5%)
  between operations  14.1 us (4%)
  other arithmetic  10 us (3%)
    all_to_all x1, blocking collectives, local(): lax.all_to_all(spread, 'section', split_axis=0, concat_axis=0, tiled=True)  125 us
    all_to_all x1, blocking collectives, local(): lax.all_to_all(send, 'expert', split_axis=0, concat_axis=0, tiled=True)  99 us
    all_to_all x1, blocking collectives, local(): lax.all_to_all(returning, 'expert', split_axis=0, concat_axis=0, tiled=True)  38.6 us
    unnamed x14, local copies, waits for them, and re-layouts  9.35 us
    psum x1, blocking collectives, local(): grad_gates = lax.psum(gate_share, 'section')  9.2 us
    dot_general x1, matrix products, local(): jnp.einsum('srd,hsd->rh', gathered, w_local, preferred_element_type=jnp.f...  7.7 us
  transfers between devices with their start and end apart: 1, of which 0 were waited for; matrix products, arithmetic and copies ran while one was open for 3% of the time, Pallas kernels for 0%

commit v1 on v0

--- a/solution.py
+++ b/solution.py
@@ -1,7 +1,15 @@
+import functools
 import jax
 import jax.numpy as jnp
 from jax import lax
 from jax.sharding import PartitionSpec as P
+
+
+def prepare_the_shifts_all(arr, mesh_dim):
+    return jax.lax.all_gather(arr, axis_name=mesh_dim).sum(axis=0)
+
+
+create_cubes = functools.partial(prepare_the_shifts_all, mesh_dim="section")
 
 
 def routing(expert_ids, experts, capacity):
@@ -66,7 +74,7 @@
     ).reshape(tok_count, top_count, hidden_slice)
     grad_hidden = (gate_weights[:, :, None] * unscaled_tok).astype(jnp.bfloat16)
     gate_share = jnp.sum(act.astype(jnp.float32) * unscaled_tok, axis=2)
-    grad_gates = lax.psum(gate_share, "section")
+    grad_gates = create_cubes(gate_share)
     return (grad_hidden, grad_gates, grad_w)
 
 

time: 340 us -> 343 us (level)
    all_gather x0 -> x1, blocking collectives: none -> 12 us  [prepare_the_shifts_all(): return jax.lax.all_gather(arr, axis_name=mesh_dim).sum(axis=0)]
    psum x1 -> x0, blocking collectives: 9.2 us -> none  [local(): grad_gates = lax.psum(gate_share, 'section')]
  transfers between devices with their start and end apart: 1 -> 1, of which waited for: 0 -> 0; matrix products, arithmetic and copies ran while one was open for 3% -> 4% of each run, Pallas kernels for 0% -> 0%
where the time goes in v1:
time: 343 us
  blocking collectives  275 us (80%)
  local copies, waits for them, and re-layouts  25.7 us (7%)
  matrix products  17.1 us (5%)
  between operations  14.1 us (4%)
  other arithmetic  10.6 us (3%)
    all_to_all x1, blocking collectives, local(): lax.all_to_all(spread, 'section', split_axis=0, concat_axis=0, tiled=True)  125 us
    all_to_all x1, blocking collectives, local(): lax.all_to_all(send, 'expert', split_axis=0, concat_axis=0, tiled=True)  99 us
    all_to_all x1, blocking collectives, local(): lax.all_to_all(returning, 'expert', split_axis=0, concat_axis=0, tiled=True)  38.6 us
    all_gather x1, blocking collectives, prepare_the_shifts_all(): return jax.lax.all_gather(arr, axis_name=mesh_dim).sum(axis=0)  12 us
    unnamed x14, local copies, waits for them, and re-layouts  9.35 us
    dot_general x1, matrix products, local(): jnp.einsum('srd,hsd->rh', gathered, w_local, preferred_element_type=jnp.f...  7.7 us
  transfers between devices with their start and end apart: 1, of which 0 were waited for; matrix products, arithmetic and copies ran while one was open for 4% of the time, Pallas kernels for 0%

profile of v1, /device:TPU:16, one launch (start us, length us, event | category | flops | bytes accessed | tf_op | source)
XLA Modules:
  0.0 342.5 jit_solution(9530078264517998256)
XLA Ops:
  7.2 0.0 copy-start
  7.2 0.0 copy-start.5
  7.2 0.0 copy-start.4
  7.2 0.0 reduce-scatter.2.cloned.1.call-start
  7.2 0.8 fusion.14
  8.1 0.1 fusion.15
  8.2 0.7 select_reduce_fusion
  9.0 0.7 convert_add_fusion
  9.6 5.6 %fusion.3 = pred[1536,128]{1,0:T(8,128)(4,1)S(1)} fusion(s32[128,8]{0,1:T(8,128)S(1)} %convert_add_fusion), kind=kLoop, calls=%fused_computation.5 | loop fusion | flops 2949120 | bytes 200704 | tf_op jit(solution)/shard_map/reduce_or | solution.py:26
  15.2 0.1 copy.39
  15.3 0.1 eq.70
  15.4 0.0 copy-done
  15.4 0.9 convolution_convert_fusion
  16.4 0.0 copy-done.5
  16.4 0.0 copy-done.4
  16.4 0.2 fusion.10
  16.6 1.6 fusion.8
  18.2 2.0 pad_maximum_fusion
  20.2 5.8 %copy.42 = bf16[1536,1152]{1,0:T(8,128)(2,1)} copy(bf16[1536,1152]{0,1:T(8,128)(2,1)} %pad_maximum_fusion) | data formatting | bytes 7077888 | tf_op jit(solution)/shard_map/concatenate | solution.py:50
  26.0 99.0 %all_to_all.15 = bf16[64,24,1152]{2,1,0:T(8,128)(2,1)S(1)} all-to-all(bf16[64,24,1152]{2,1,0:T(8,128)(2,1)} %bitcast.31), channel_id=1, replica_groups=mesh['dp'=2,'section'=4,'expert'=64] {'expert'}, dimensions={0} | all-to-all | bytes 7077888 | tf_op jit(solution)/shard_map/all_to_all | solution.py:53
  125.0 0.0 copy-start.1
  125.0 1.9 copy-done.1
  126.8 0.2 slice.8
  127.0 5.0 %broadcast_in_dim.16 = bf16[4,1536,896]{2,1,0:T(8,128)(2,1)} broadcast(bf16[1536,896]{1,0:T(8,128)(2,1)S(1)} %slice.8), dimensions={1,2} | broadcast | bytes 13762560 | tf_op jit(solution)/shard_map/broadcast_in_dim | solution.py:57
  132.0 125.3 %all_to_all.16 = bf16[4,1536,896]{2,1,0:T(8,128)(2,1)S(1)} all-to-all(bf16[4,1536,896]{2,1,0:T(8,128)(2,1)} %broadcast_in_dim.16), channel_id=1, replica_groups=mesh['dp'=2,'section'=4,'expert'=64] {'section'}, dimensions={0} | all-to-all | bytes 22020096 | tf_op jit(solution)/shard_map/all_to_all | solution.py:58
  257.4 0.0 copy-start.2
  257.4 4.2 %copy-done.2 = bf16[4,1536,896]{2,1,0:T(8,128)(2,1)} copy-done((bf16[4,1536,896]{2,1,0:T(8,128)(2,1)}, bf16[4,1536,896]{2,1,0:T(8,128)(2,1)S(1)}, u32[]{:S(2)}) %copy-start.2) | copy-done | bytes 11010072
  261.5 5.3 %convolution_convert_fusion.1 = bf16[256,4,896]{2,0,1:T(8,128)(2,1)} fusion(bf16[4,1536,896]{2,1,0:T(8,128)(2,1)S(1)} %all_to_all.16, bf16[1536,1152]{1,0:T(8,128)(2,1)} %bitcast.33), kind=kOutput, calls=%fused_computation.15 | convolution fusion | flops 2819489792 | bytes 13631488 | tf_op jit(solution)/shard_map/rh,srd->hsd/dot_general | solution.py:62
  266.8 0.0 copy-start.3
  266.8 3.7 %copy.45 = bf16[256,4,896]{0,2,1:T(8,128)(2,1)} copy(bf16[256,4,896]{2,0,1:T(8,128)(2,1)} %convolution_convert_fusion.1) | data formatting | bytes 3670016 | tf_op jit(solution)/shard_map/convert_element_type | solution.py:63
  270.5 0.0 reduce-scatter.2.cloned.1.call-update
  270.6 0.0 copy-done.3
  270.6 1.5 reshape_squeeze.3
  272.1 7.7 %fusion.7 = bf16[1536,256]{1,0:T(8,128)(2,1)S(1)} fusion(bf16[4,1536,896]{2,1,0:T(8,128)(2,1)} %copy-done.2, bf16[256,4,896]{2,1,0:T(4,128)(2,1)} %reshape_squeeze.3), kind=kOutput, calls=%fused_computation.12 | convolution fusion | flops 2818965504 | bytes 13631488 | tf_op jit(solution)/shard_map/srd,hsd->rh/dot_general | solution.py:60
  279.8 38.6 %all_to_all.17 = bf16[64,24,256]{2,1,0:T(8,128)(2,1)S(1)} all-to-all(bf16[64,24,256]{2,1,0:T(8,128)(2,1)S(1)} %bitcast.36), channel_id=1, replica_groups=mesh['dp'=2,'section'=4,'expert'=64] {'expert'}, dimensions={0} | all-to-all | bytes 1572864 | tf_op jit(solution)/shard_map/all_to_all | solution.py:68
  318.4 1.4 fusion.11
  319.8 1.1 copy.46
  320.9 12.0 %all-gather = f32[512,8]{0,1:T(8,128)S(1)} all-gather(f32[128,8]{0,1:T(8,128)S(1)} %get-tuple-element.15), channel_id=2, replica_groups=mesh['dp'=2,'section'=4,'expert'=64] {'section'}, dimensions={0}, use_global_device_ids=true | all-gather | bytes 20480 | tf_op jit(solution)/shard_map/all_gather | solution.py:9
  332.9 0.6 bitcast_reduce_fusion
  333.5 0.0 reduce-scatter.2.cloned.1.call-done
  333.5 2.2 copy.47
Async XLA Ops:
  7.2 8.3 %copy-start = (bf16[128,896]{1,0:T(8,128)(2,1)S(1)}, bf16[128,896]{1,0:T(8,128)(2,1)}, u32[]{:S(2)}) copy-start(bf16[128,896]{1,0:T(8,128)(2,1)} %param.5) | copy-start | bytes 688132
  7.2 9.2 %copy-start.5 = (f32[128,8]{0,1:T(8,128)S(1)}, f32[128,8]{0,1:T(8,128)}, u32[]{:S(2)}) copy-start(f32[128,8]{0,1:T(8,128)} %param.7) | copy-start | bytes 12292
  7.2 9.2 %copy-start.4 = (bf16[128,8,256]{2,1,0:T(8,128)(2,1)S(1)}, bf16[128,8,256]{2,1,0:T(8,128)(2,1)}, u32[]{:S(2)}) copy-start(bf16[128,8,256]{2,1,0:T(8,128)(2,1)} %param.8) | copy-start | bytes 1572868
  7.2 326.3 %reduce-scatter.2.cloned.1.call-start = ((), (), s32[]{:S(2)}) async-start(), calls=%async_computation.4 | async-start | bytes 2752512 | tf_op jit(solution)/shard_map/reduce_scatter | solution.py:66
  125.0 1.9 copy-start.1
  257.4 4.2 %copy-start.2 = (bf16[4,1536,896]{2,1,0:T(8,128)(2,1)}, bf16[4,1536,896]{2,1,0:T(8,128)(2,1)S(1)}, u32[]{:S(2)}) copy-start(bf16[4,1536,896]{2,1,0:T(8,128)(2,1)S(1)} %all_to_all.16) | copy-start | bytes 33030148
  266.8 3.7 %copy-start.3 = (bf16[1,256,3584]{2,1,0:T(8,128)(2,1)S(1)}, bf16[1,256,3584]{2,1,0:T(8,128)(2,1)}, u32[]{:S(2)}) copy-start(bf16[1,256,3584]{2,1,0:T(8,128)(2,1)} %param.9) | copy-start | bytes 5505028
Sparse Core Ops, SparseCore 0:
  270.7 19.9 reduce-scatter.1
